TPU v7x, 256 devices: a whole 4x4x8 slice. The times are simulated.
256 devices in a mesh: group: 32 (over z, y), tensor: 8 (over x, core).
Axes of the slice: x: 4, y: 4, z: 8, core: 2. Of those that a mesh axis runs over, the one named last changes fastest.
Arguments:
- query: bfloat16 [2, 1024, 2048], P(None, 'group', 'tensor'), may hold values from -80 to 80
- self_kv: bfloat16 [2, 1024, 2, 2048], P(None, 'group', None, 'tensor'), may hold values from -6 to 6
- kv_pages: bfloat16 [2, 1536, 16, 2, 2048], P(None, 'group', None, None, 'tensor'), may hold values from -6 to 6
- page_dest: int32 [1536, 1], replicated, may hold values from 0 to 31; in each aligned block of 48 rows (0 to 47, 48 to 95, ...) at most 3 rows name the same one
- page_request: int32 [1536], replicated, may hold values from 0 to 1
- score_len: int32 [64], P('group'), may hold values from 1 to 16
- out_proj: bfloat16 [2, 2048, 2048], P(None, 'tensor'), may hold values from -0.125 to 0.125
- residual: bfloat16 [2, 1024, 2048], P(None, ('group', 'tensor')), may hold values from -6 to 6
- norm_gain: float32 [2, 2048], replicated, may hold values from 0.5 to 40
- norm_bias: float32 [2, 2048], replicated, may hold values from -3 to 3
- vocab: bfloat16 [2, 2048, 196608], P(None, None, ('group', 'tensor')), may hold values from -0.3984375 to 0.3984375
- targets: int32 [1024], replicated, may hold values from 0 to 196607
Outputs:
- logprob: float32 [2, 1024], P(None, ('group', 'tensor'))
Inputs may be any that keep to these rules, and one draw needn't show every extreme that they name: `page_dest`: the 48 pages of each aligned block (pages held by one group) go to any one group at most 3 times; some block sends exactly 3 to some group.
All inputs are finite; a program needn't handle non-finite values.
Results may differ from a plain program's by a relative error of at most 0.00097.
Values may be sent and summed in bfloat16 or wider, within the bound.
No kernel may reach another device: no remote copies, remote signals or barrier semaphores. Data moves between devices by JAX's collectives and lax.ppermute only.
A program may use at most 128 MiB of HBM per device.

v0:
```python
import math

import jax
import jax.numpy as jnp
from jax import lax
from jax.sharding import PartitionSpec as P

HEADS = 16
HEAD_DIM = 128
REQ_GRP = 2
SCORE_LEN = 16


NEGATIVE = -1e30
EPSILON = 1e-05


def alibi_slopes(head_count):
    return jnp.exp2(-8.0 * jnp.arange(1, head_count + 1).astype(jnp.float32) / head_count)


def lse_combine(peak, total, chosen, axis):
    top = jnp.max(peak, axis=axis, keepdims=True)
    total = jnp.sum(total * jnp.exp(peak - top), axis=axis)
    return jnp.squeeze(top, axis), total, jnp.sum(chosen, axis=axis)


def per_device(
    query,
    self_kv,
    kv_pages,
    page_dest,
    page_request,
    score_len,
    out_proj,
    residual,
    norm_gain,
    norm_bias,
    vocab,
    targets,
):
    groups = lax.axis_size("group")
    shards = lax.axis_size("tensor")
    group_id = lax.axis_index("group")
    tensor_id = lax.axis_index("tensor")
    tok_grp = query.shape[1]
    flat_width = query.shape[2]
    head_local = flat_width // HEAD_DIM
    per_owner = kv_pages.shape[1]
    page_len = kv_pages.shape[2]
    capacity = 2 * per_owner // groups
    destination = page_dest[:, 0]
    page_total = destination.shape[0]
    buffer = groups * capacity
    width = residual.shape[2]

    local = jnp.arange(per_owner, dtype=jnp.int32)
    earlier = local[None, :] < local[:, None]
    my_dest = lax.dynamic_slice_in_dim(destination, group_id * per_owner, per_owner)
    my_position = jnp.sum(
        ((my_dest[None, :] == my_dest[:, None]) & earlier).astype(jnp.int32), axis=1
    )
    out_slot = my_dest * capacity + my_position
    slots = jnp.arange(buffer, dtype=jnp.int32)
    send_hot = (out_slot[None, :] == slots[:, None]).astype(kv_pages.dtype)
    outgoing = jnp.einsum(
        "sp,mpjcx->scmjx", send_hot, kv_pages, preferred_element_type=jnp.float32
    ).astype(kv_pages.dtype)
    incoming = lax.all_to_all(
        outgoing.reshape(buffer, -1, flat_width), "group", split_axis=0, concat_axis=0, tiled=True
    ).reshape(outgoing.shape)

    pages = jnp.arange(page_total, dtype=jnp.int32)
    mine = destination == group_id
    mine_blocks = mine.reshape(groups, per_owner)
    rank_in_block = jnp.sum(
        (mine_blocks[:, None, :] & earlier[None]).astype(jnp.int32), axis=2
    ).reshape(-1)
    arrival = (pages // per_owner) * capacity + rank_in_block
    recv_hot = mine[None, :] & (arrival[None, :] == slots[:, None])
    is_valid = jnp.any(recv_hot, axis=1)
    slot_page = jnp.sum(jnp.where(recv_hot, pages[None, :], 0), axis=1)
    slot_request = jnp.sum(jnp.where(recv_hot, page_request[None, :], 0), axis=1)
    slot_rank = jnp.sum(
        (
            mine[None, :]
            & (page_request[None, :] == slot_request[:, None])
            & (pages[None, :] < slot_page[:, None])
        ).astype(jnp.int32),
        axis=1,
    )
    request_ids = jnp.arange(REQ_GRP, dtype=jnp.int32)
    totals = jnp.sum(
        (mine[None, :] & (page_request[None, :] == request_ids[:, None])).astype(jnp.int32),
        axis=1,
    )

    slopes = lax.dynamic_slice_in_dim(alibi_slopes(HEADS), tensor_id * head_local, head_local)
    score_scale = 1.0 / math.sqrt(HEAD_DIM)
    token_ids = jnp.arange(tok_grp, dtype=jnp.int32)
    token_request = token_ids // SCORE_LEN
    token_step = token_ids % SCORE_LEN
    own_distance = (token_step[:, None] - token_step[None, :]).astype(jnp.float32)
    own_allowed = (
        (token_request[:, None] == token_request[None, :])
        & (token_step[None, :] <= token_step[:, None])
    )[None]
    key_request = jnp.repeat(jnp.where(is_valid, slot_request, -1), page_len)
    key_position = (
        slot_rank[:, None] * page_len + jnp.arange(page_len, dtype=jnp.int32)[None, :]
    ).reshape(-1)
    context = totals[token_request] * page_len
    distance = ((context + token_step)[:, None] - key_position[None, :]).astype(jnp.float32)
    allowed = (key_request[None, :] == token_request[:, None])[None]
    page_keys = incoming[:, 0]
    page_values = incoming[:, 1]
    heads_out = []
    for h in range(head_local):
        lanes_h = slice(h * HEAD_DIM, (h + 1) * HEAD_DIM)
        q = query[:, :, lanes_h]
        own_k = self_kv[:, :, 0, lanes_h]
        own_v = self_kv[:, :, 1, lanes_h]
        slope = slopes[h]
        own_scores = (
            jnp.einsum("mtd,msd->mts", q, own_k, preferred_element_type=jnp.float32) * score_scale
        )
        own_scores = own_scores - slope * own_distance[None]
        own_scores = jnp.where(own_allowed, own_scores, NEGATIVE)
        scores = (
            jnp.einsum("mtd,smjd->mtsj", q, page_keys[..., lanes_h],
                       preferred_element_type=jnp.float32).reshape(2, tok_grp, -1) * score_scale
        )
        scores = scores - slope * distance[None]
        scores = jnp.where(allowed, scores, NEGATIVE)
        row_top = jnp.maximum(jnp.max(scores, -1), jnp.max(own_scores, -1))
        exp_terms = jnp.where(allowed, jnp.exp(scores - row_top[..., None]), 0.0)
        own_terms = jnp.where(own_allowed, jnp.exp(own_scores - row_top[..., None]), 0.0)
        denominator = jnp.sum(exp_terms, -1) + jnp.sum(own_terms, -1)
        numerator = jnp.einsum(
            "mtsj,smjd->mtd",
            exp_terms.astype(jnp.bfloat16).reshape(2, tok_grp, buffer, page_len),
            page_values[..., lanes_h],
            preferred_element_type=jnp.float32,
        ) + jnp.einsum(
            "mts,msd->mtd", own_terms.astype(jnp.bfloat16), own_v,
            preferred_element_type=jnp.float32,
        )
        heads_out.append(numerator / denominator[..., None])
    attended = jnp.concatenate(heads_out, axis=-1).astype(jnp.bfloat16)

    rows_local = tok_grp // shards
    side = tensor_id % 2
    x_size = shards // 2
    x_id = tensor_id // 2
    swap = [(t, t ^ 1) for t in range(shards)]

    def x_shift(step):
        return [(t, (t + 2 * step) % shards) for t in range(shards)]

    partial = jnp.einsum("mtk,mkd->tmd", attended, out_proj, preferred_element_type=jnp.float32)
    partial = partial.reshape(x_size, 2, rows_local, 2, width)
    own_rows = jnp.transpose(residual.astype(jnp.float32), (1, 0, 2))
    partial = lax.dynamic_update_slice(
        partial,
        (lax.dynamic_slice(partial, (x_id, side, 0, 0, 0), (1, 1, rows_local, 2, width))
         + own_rows[None, None]),
        (x_id, side, 0, 0, 0),
    )
    pair_sum = lax.dynamic_index_in_dim(partial, side, 1, keepdims=False) + lax.ppermute(
        lax.dynamic_index_in_dim(partial, 1 - side, 1, keepdims=False), "tensor", swap
    )
    hidden = pair_sum
    for k in range(1, x_size):
        hidden = hidden + lax.ppermute(pair_sum, "tensor", x_shift(k))
    hidden = jnp.transpose(hidden.reshape(x_size * rows_local, 2, width), (1, 0, 2))
    row_mean = jnp.mean(hidden, axis=-1, keepdims=True)
    centered = hidden - row_mean
    variance = jnp.mean(centered * centered, axis=-1, keepdims=True)
    normed = (
        centered / jnp.sqrt(variance + EPSILON) * norm_gain[:, None, :] + norm_bias[:, None, :]
    ).astype(jnp.bfloat16)

    voc_local = vocab.shape[2]
    offset = (group_id * shards + tensor_id) * voc_local
    y_size = 4
    z_size = groups // y_size
    z_id = group_id // y_size
    y_id = group_id % y_size
    kept = lax.dynamic_index_in_dim(normed, side, 0, keepdims=False).reshape(x_size, rows_local, width)
    given = lax.ppermute(
        lax.dynamic_index_in_dim(normed, 1 - side, 0, keepdims=False), "tensor", swap
    ).reshape(x_size, rows_local, width)
    block = jnp.where(
        side == 0, jnp.stack([kept, given], 1), jnp.stack([given, kept], 1)
    ).reshape(tok_grp, width)

    def y_shift(step):
        return [(z * y_size + y, z * y_size + (y + step) % y_size)
                for z in range(z_size) for y in range(y_size)]

    def z_shift(step):
        return [(z * y_size + y, ((z + step) % z_size) * y_size + y)
                for z in range(z_size) for y in range(y_size)]

    block = jnp.concatenate(
        [block] + [lax.ppermute(block, "group", y_shift(k)) for k in range(1, y_size)], 0
    )
    forward, backward = block, block
    chunks = [block]
    z_from = [0]
    for k in range(1, z_size // 2):
        forward = lax.ppermute(forward, "group", z_shift(1))
        chunks.append(forward)
        z_from.append(k)
        backward = lax.ppermute(backward, "group", z_shift(z_size - 1))
        chunks.append(backward)
        z_from.append(z_size - k)
    split = block.shape[0] // 2
    chunks.append(jnp.concatenate([
        lax.ppermute(forward[:split], "group", z_shift(1)),
        lax.ppermute(backward[split:], "group", z_shift(z_size - 1)),
    ], 0))
    z_from.append(z_size // 2)
    own_model = jnp.concatenate(chunks, 0)
    other_model = lax.ppermute(own_model, "tensor", swap)
    z_from = jnp.array(z_from, dtype=jnp.int32)
    y_from = jnp.arange(y_size, dtype=jnp.int32)
    source_group = (
        ((z_id - z_from[:, None]) % z_size) * y_size + (y_id - y_from[None, :]) % y_size
    ).reshape(-1)
    wanted = (targets.reshape(groups, tok_grp)[source_group] - offset).reshape(-1)
    lanes = jnp.arange(voc_local, dtype=jnp.int32)

    def local_stats(rows, weights):
        logits = jnp.dot(rows, weights, preferred_element_type=jnp.float32)
        peak = jnp.max(logits, axis=1)
        total = jnp.sum(jnp.exp(logits - peak[:, None]), axis=1)
        chosen = jnp.sum(jnp.where(lanes[None, :] == wanted[:, None], logits, 0.0), axis=1)
        return jnp.stack([peak, total, chosen])

    own_stats = local_stats(own_model, lax.dynamic_index_in_dim(vocab, side, 0, keepdims=False))
    other_stats = local_stats(
        other_model, lax.dynamic_index_in_dim(vocab, 1 - side, 0, keepdims=False)
    )
    stats = jnp.where(
        side == 0, jnp.stack([own_stats, other_stats], 1), jnp.stack([other_stats, own_stats], 1)
    ).reshape(3, 2, groups, tok_grp)
    group_at = jnp.zeros((groups,), jnp.int32).at[source_group].set(
        jnp.arange(groups, dtype=jnp.int32)
    )
    stats = jnp.take(stats, group_at, axis=2)
    stats = stats.reshape(3, 2, groups, shards, rows_local)

    stats = lax.all_to_all(stats, "tensor", 3, 3, tiled=True)
    peak, total, chosen = lse_combine(stats[0], stats[1], stats[2], 2)
    stats = lax.all_to_all(jnp.stack([peak, total, chosen]), "group", 2, 2, tiled=True)
    peak, total, chosen = lse_combine(stats[0], stats[1], stats[2], 1)
    mine_lp = chosen - (peak + jnp.log(total))

    local_ids = tensor_id * rows_local + jnp.arange(rows_local, dtype=jnp.int32)
    keep_token = local_ids % SCORE_LEN < score_len[local_ids // SCORE_LEN]
    return jnp.where(keep_token[None, :], mine_lp, 0.0)


def solution(mesh):
    in_specs = (
        P(None, "group", "tensor"),
        P(None, "group", None, "tensor"),
        P(None, "group", None, None, "tensor"),
        P(),
        P(),
        P("group"),
        P(None, "tensor", None),
        P(None, ("group", "tensor"), None),
        P(),
        P(),
        P(None, None, ("group", "tensor")),
        P(),
    )
    out_specs = P(None, ("group", "tensor"))
    return jax.shard_map(
        per_device, mesh=mesh, in_specs=in_specs, out_specs=out_specs, check_vma=False
    )
```

profile of v0, /device:TPU:1, one launch (start us, length us, event | category | flops | bytes accessed | tf_op | source)
XLA Modules:
  0.0 236.9 jit_solution(5202914442172681584)
XLA Ops:
  0.0 0.9 fusion.84
  1.1 0.8 multiply_add_fusion
  1.8 2.8 %convert_bitcast_fusion = bf16[96,2,2,16,256]{4,0,1,3,2:T(8,128)(2,1)S(1)} fusion(bf16[2,48,16,2,256]{4,3,2,1,0:T(2,128)(2,1)} %param.15, s32[48]{0:T(128)S(1)} %multiply_add_fusion), kind=kOutput, calls=%fused_computation.15 | convolution fusion | flops 152572416 | bytes 4718784 | tf_op jit(solution)/shard_map/sp,mpjcx->scmjx/dot_general | solution.py:66
  4.6 3.5 %copy.64 = bf16[96,2,2,16,256]{4,3,2,1,0:T(8,128)(2,1)} copy(bf16[96,2,2,16,256]{4,0,1,3,2:T(8,128)(2,1)S(1)} %convert_bitcast_fusion) | data formatting | bytes 6291456 | tf_op jit(solution)/shard_map/convert_element_type | solution.py:68
  8.1 12.3 %all-to-all-start = ((bf16[96,64,256]{2,1,0:T(8,128)(2,1)}), bf16[96,64,256]{2,1,0:T(8,128)(2,1)}, u32[]{:S(2)}, u32[]{:S(2)}) async-start(bf16[96,64,256]{2,1,0:T(8,128)(2,1)} %bitcast.162), calls=%async_computation | async-start | bytes 6291456 | tf_op jit(solution)/shard_map/all_to_all | solution.py:69
  20.6 0.6 convert_reduce_fusion
  21.5 0.6 fusion.97
  22.1 1.2 fusion.81
  23.3 0.6 fusion.96
  24.8 1.4 convert_multiply_fusion.3
  26.8 2.4 %convert_multiply_fusion.1 = (f32[32,96,16]{0,2,1:T(8,128)}, f32[32,96,16]{0,2,1:T(8,128)S(1)}) fusion(s32[96,16]{1,0:T(8,128)S(1)} %iota_add_fusion, s32[32]{0:T(128)S(1)} %fusion.81, f32[]{:T(128)} %bitcast.12, f32[]{:T(128)} %bitcast.24), kind=kLoop, calls=%fused_computation.53 | loop fusion | flops 196608 | bytes 399496 | tf_op jit(solution)/shard_map/mul | solution.py:133
  29.3 61.7 %all-to-all-done = bf16[96,64,256]{2,1,0:T(8,128)(2,1)} async-done(((bf16[96,64,256]{2,1,0:T(8,128)(2,1)}), bf16[96,64,256]{2,1,0:T(8,128)(2,1)}, u32[]{:S(2)}, u32[]{:S(2)}) %all-to-all-start) | async-done | bytes 3145760 | tf_op jit(solution)/shard_map/all_to_all | solution.py:69
  91.0 2.2 fusion.94
  93.5 0.8 copy-done.2
  95.9 0.7 fusion.9
  98.4 2.7 %collective-permute-start = (f32[4,4,2,2048]{3,1,0,2:T(4,128)S(1)}, f32[4,4,2,2048]{3,1,0,2:T(4,128)S(1)}, u32[]{:S(2)}, u32[]{:S(2)}) collective-permute-start(f32[4,4,2,2048]{3,1,0,2:T(4,128)S(1)} %dynamic-slice_bitcast_fusion), channel_id=1, source_target_pairs={{0,1},{1,0},{2,3},{3,2},{4,5},{5,4},{6,7},{7,6},{8,9},{9,8},{10,11... | collective-permute-start | bytes 786440 | tf_op jit(solution)/shard_map/ppermute | solution.py:169
  101.1 1.2 collective-permute-done
  102.3 2.6 %collective-permute-start.3 = (f32[4,4,2,2048]{3,1,0,2:T(4,128)S(1)}, f32[4,4,2,2048]{3,1,0,2:T(4,128)S(1)}, u32[]{:S(2)}, u32[]{:S(2)}) collective-permute-start(f32[4,4,2,2048]{3,1,0,2:T(4,128)S(1)} %bitcast_add_fusion), channel_id=1, source_target_pairs={{0,6},{1,7},{2,0},{3,1},{4,2},{5,3},{6,4},{7,5},{8,14},{9,15},{10,... | collective-permute-start | bytes 786440 | tf_op jit(solution)/shard_map/ppermute | solution.py:174
  105.4 0.6 collective-permute-start.1
  106.0 9.7 %collective-permute-done.3 = f32[4,4,2,2048]{3,1,0,2:T(4,128)S(1)} collective-permute-done((f32[4,4,2,2048]{3,1,0,2:T(4,128)S(1)}, f32[4,4,2,2048]{3,1,0,2:T(4,128)S(1)}, u32[]{:S(2)}, u32[]{:S(2)}) %collective-permute-start.3) | collective-permute-done | bytes 262176 | tf_op jit(solution)/shard_map/ppermute | solution.py:174
  115.7 4.6 %collective-permute-done.1 = f32[4,4,2,2048]{3,1,0,2:T(4,128)S(1)} collective-permute-done((f32[4,4,2,2048]{3,1,0,2:T(4,128)S(1)}, f32[4,4,2,2048]{3,1,0,2:T(4,128)S(1)}, u32[]{:S(2)}, u32[]{:S(2)}) %collective-permute-start.1) | collective-permute-done | bytes 262176 | tf_op jit(solution)/shard_map/ppermute | solution.py:174
  120.9 0.6 collective-permute-start.4
  121.5 0.9 collective-permute-done.4
  123.1 2.4 %collective-permute-start.6 = (bf16[32,2048]{1,0:T(8,128)(2,1)S(1)}, bf16[32,2048]{1,0:T(8,128)(2,1)S(1)}, u32[]{:S(2)}, u32[]{:S(2)}) collective-permute-start(bf16[32,2048]{1,0:T(8,128)(2,1)S(1)} %select_n.304), channel_id=1, source_target_pairs={{0,16},{8,24},{16,0},{24,8},{32,48},{40,56},{48,32},{56,40},{64,80... | collective-permute-start | bytes 393224 | tf_op jit(solution)/shard_map/ppermute | solution.py:206
  125.5 1.1 collective-permute-start.7
  126.5 0.7 constant_dynamic-update-slice_fusion.3
  127.2 1.4 collective-permute-done.5
  128.6 0.7 constant_dynamic-update-slice_fusion.2
  129.2 2.3 collective-permute-done.6
  131.5 0.7 constant_dynamic-update-slice_fusion.1
  132.2 0.7 constant_dynamic-update-slice_fusion
  132.9 2.1 collective-permute-start.8
  135.0 0.6 collective-permute-start.9
  135.6 10.8 %collective-permute-done.8 = bf16[128,2048]{1,0:T(8,128)(2,1)S(1)} collective-permute-done((bf16[128,2048]{1,0:T(8,128)(2,1)S(1)}, bf16[128,2048]{1,0:T(8,128)(2,1)S(1)}, u32[]{:S(2)}, u32[]{:S(2)}) %collective-permute-start.8) | collective-permute-done | bytes 524320 | tf_op jit(solution)/shard_map/ppermute | solution.py:212
  146.3 0.9 collective-permute-start.10
  147.2 1.8 collective-permute-start.11
  149.0 0.9 constant_dynamic-update-slice_fusion.11
  149.9 9.0 %collective-permute-done.10 = bf16[128,2048]{1,0:T(8,128)(2,1)S(1)} collective-permute-done((bf16[128,2048]{1,0:T(8,128)(2,1)S(1)}, bf16[128,2048]{1,0:T(8,128)(2,1)S(1)}, u32[]{:S(2)}, u32[]{:S(2)}) %collective-permute-start.10) | collective-permute-done | bytes 524320 | tf_op jit(solution)/shard_map/ppermute | solution.py:212
  158.9 2.7 %collective-permute-start.13 = (bf16[128,2048]{1,0:T(8,128)(2,1)S(1)}, bf16[128,2048]{1,0:T(8,128)(2,1)S(1)}, u32[]{:S(2)}, u32[]{:S(2)}) collective-permute-start(bf16[128,2048]{1,0:T(8,128)(2,1)S(1)} %collective-permute-done.11), channel_id=1, source_target_pairs={{0,224},{8,232},{16,240},{24,248},{32,0},{40,8},{48,16},{56,24},{6... | collective-permute-start | bytes 1572872 | tf_op jit(solution)/shard_map/ppermute | solution.py:215
  161.5 0.8 constant_dynamic-update-slice_fusion.10
  162.4 0.8 constant_dynamic-update-slice_fusion.9
  163.2 0.8 constant_dynamic-update-slice_fusion.8
  164.1 6.4 %collective-permute-done.12 = bf16[128,2048]{1,0:T(8,128)(2,1)S(1)} collective-permute-done((bf16[128,2048]{1,0:T(8,128)(2,1)S(1)}, bf16[128,2048]{1,0:T(8,128)(2,1)S(1)}, u32[]{:S(2)}, u32[]{:S(2)}) %collective-permute-start.12) | collective-permute-done | bytes 524320 | tf_op jit(solution)/shard_map/ppermute | solution.py:212
  170.6 2.7 %collective-permute-start.15 = (bf16[64,2048]{1,0:T(8,128)(2,1)S(1)}, bf16[64,2048]{1,0:T(8,128)(2,1)S(1)}, u32[]{:S(2)}, u32[]{:S(2)}) collective-permute-start(bf16[64,2048]{1,0:T(8,128)(2,1)S(1)} %slice.104), channel_id=1, source_target_pairs={{0,224},{8,232},{16,240},{24,248},{32,0},{40,8},{48,16},{56,24},{6... | collective-permute-start | bytes 786440 | tf_op jit(solution)/shard_map/ppermute | solution.py:221
  173.3 0.9 constant_dynamic-update-slice_fusion.7
  174.2 0.8 constant_dynamic-update-slice_fusion.6
  175.0 2.0 collective-permute-done.14
  177.0 0.7 constant_dynamic-update-slice_fusion.5
  177.7 0.7 constant_dynamic-update-slice_fusion.4
  178.4 5.1 %collective-permute-start.16 = (bf16[1024,2048]{1,0:T(8,128)(2,1)}, bf16[1024,2048]{1,0:T(8,128)(2,1)}, u32[]{:S(2)}, u32[]{:S(2)}) collective-permute-start(bf16[1024,2048]{1,0:T(8,128)(2,1)} %constant_dynamic-update-slice_fusion.4), channel_id=1, source_target_pairs={{0,1},{1,0},{2,3},{3,2},{4,5},{5,4},{6,7},{7,6},{8,9},{9,8},{10,11... | collective-permute-start | bytes 12582920 | tf_op jit(solution)/shard_map/ppermute | solution.py:225
  183.8 0.9 scatter_custom_fusion
  185.4 8.4 %fusion.103 = (f32[1024]{0:T(1024)S(1)}, f32[1024,768]{0,1:T(8,128)}) fusion(bf16[1024,2048]{1,0:T(8,128)(2,1)} %constant_dynamic-update-slice_fusion.4, bf16[2,2048,768]{2,1,0:T(8,128)(2,1)} %param.23, s32[]{:T(128)S(6)} %select_n.301), kind=kOutput, calls=%fused_computation.235 | convolution fusion | flops 3222010880 | bytes 10489860 | tf_op jit(solution)/shard_map/dot_general | solution.py:235
  193.9 8.3 %fusion.102 = (f32[1024]{0:T(1024)S(1)}, f32[1024,768]{0,1:T(8,128)}) fusion(bf16[1024,2048]{1,0:T(8,128)(2,1)} %collective-permute-done.16, bf16[2,2048,768]{2,1,0:T(8,128)(2,1)} %param.23, s32[]{:T(128)S(6)} %select_n.302), kind=kOutput, calls=%fused_computation.234 | convolution fusion | flops 3222010880 | bytes 10489860 | tf_op jit(solution)/shard_map/dot_general | solution.py:235
  202.3 4.4 %select_reduce_fusion.1 = (f32[1024]{0:T(1024)S(1)}, f32[1024]{0:T(1024)S(1)}, f32[1024]{0:T(1024)S(1)}, f32[1024]{0:T(1024)S(1)}) fusion(f32[1024,768]{0,1:T(8,128)} %get-tuple-element.52, s32[1024]{0:T(1024)S(1)} %sub.261, f32[1024]{0:T(1024)S(1)} %get-tuple-element.51, f32[1024,768]{0,1:T(8,128)} %get-tuple-element.50, f32[1024]{0:T(1024)S(1)} %get-tuple-element.49), kind=kLoop, calls=%fused_computation.11 | loop fusion | flops 7073792 | bytes 6320128 | tf_op jit(solution)/shard_map/reduce_sum | solution.py:238
  207.3 0.7 gather_fusion.2
  208.2 0.7 reshape.703
  208.9 3.3 %all-to-all-start.1 = ((f32[8,1,768]{2,1,0:T(1,128)}), f32[8,1,768]{2,1,0:T(1,128)S(1)}, u32[]{:S(2)}, u32[]{:S(2)}) async-start(f32[8,1,768]{2,1,0:T(1,128)} %reshape.703), calls=%async_computation.1 | async-start | bytes 49152 | tf_op jit(solution)/shard_map/all_to_all | solution.py:254
  212.2 0.6 gather_fusion
  212.9 4.0 %all-to-all-done.1 = f32[8,1,768]{2,1,0:T(1,128)S(1)} async-done(((f32[8,1,768]{2,1,0:T(1,128)}), f32[8,1,768]{2,1,0:T(1,128)S(1)}, u32[]{:S(2)}, u32[]{:S(2)}) %all-to-all-start.1) | async-done | bytes 24608 | tf_op jit(solution)/shard_map/all_to_all | solution.py:254
  217.4 0.7 reduce.11
  218.3 0.7 copy.78
  219.0 8.1 %all-to-all-start.2 = ((f32[3,2,32,4]{3,1,0,2:T(2,128)}), f32[3,2,32,4]{3,1,0,2:T(2,128)S(1)}, u32[]{:S(2)}, u32[]{:S(2)}) async-start(f32[3,2,32,4]{3,1,0,2:T(2,128)} %copy.78), calls=%async_computation.2 | async-start | bytes 196608 | tf_op jit(solution)/shard_map/all_to_all | solution.py:256
  227.1 9.1 %all-to-all-done.2 = f32[3,2,32,4]{3,1,0,2:T(2,128)S(1)} async-done(((f32[3,2,32,4]{3,1,0,2:T(2,128)}), f32[3,2,32,4]{3,1,0,2:T(2,128)S(1)}, u32[]{:S(2)}, u32[]{:S(2)}) %all-to-all-start.2) | async-done | bytes 3104 | tf_op jit(solution)/shard_map/all_to_all | solution.py:256
  236.3 0.6 subtract_select_fusion
  (127 shorter events, 10.4 us)
Async XLA Ops:
  0.0 97.6 %copy-start = (bf16[2,256,2048]{2,1,0:T(8,128)(2,1)S(1)}, bf16[2,256,2048]{2,1,0:T(8,128)(2,1)}, u32[]{:S(2)}) copy-start(bf16[2,256,2048]{2,1,0:T(8,128)(2,1)} %param.19) | copy-start | bytes 6291460
  8.1 12.3 %copy-start.9 = (s32[1536,1]{0,1:T(1,128)S(1)}, s32[1536,1]{0,1:T(1,128)}, u32[]{:S(2)}) copy-start(s32[1536,1]{0,1:T(1,128)} %param.16) | copy-start | bytes 18436
  8.1 13.3 %copy-start.4 = (s32[1536]{0:T(1024)S(1)}, s32[1536]{0:T(1024)}, u32[]{:S(2)}) copy-start(s32[1536]{0:T(1024)} %param.17) | copy-start | bytes 18436
  8.1 18.1 %copy-start.3 = (bf16[2,32,2,256]{3,2,1,0:T(2,128)(2,1)S(1)}, bf16[2,32,2,256]{3,2,1,0:T(2,128)(2,1)}, u32[]{:S(2)}) copy-start(bf16[2,32,2,256]{3,2,1,0:T(2,128)(2,1)} %param.14) | copy-start | bytes 196612
  8.1 18.3 %copy-start.6 = (bf16[2,32,256]{2,1,0:T(8,128)(2,1)S(1)}, bf16[2,32,256]{2,1,0:T(8,128)(2,1)}, u32[]{:S(2)}) copy-start(bf16[2,32,256]{2,1,0:T(8,128)(2,1)} %param.13) | copy-start | bytes 98308
  8.1 82.9 %all-to-all-start = ((bf16[96,64,256]{2,1,0:T(8,128)(2,1)}), bf16[96,64,256]{2,1,0:T(8,128)(2,1)}, u32[]{:S(2)}, u32[]{:S(2)}) async-start(bf16[96,64,256]{2,1,0:T(8,128)(2,1)} %bitcast.162), calls=%async_computation | async-start | bytes 6291456 | tf_op jit(solution)/shard_map/all_to_all | solution.py:69
  93.2 1.1 copy-start.2
  96.6 1.7 copy-start.5
  98.1 22.6 %copy-start.7 = (f32[2,2048]{1,0:T(2,128)S(1)}, f32[2,2048]{1,0:T(2,128)}, u32[]{:S(2)}) copy-start(f32[2,2048]{1,0:T(2,128)} %param.22) | copy-start | bytes 49156
  98.1 22.6 %copy-start.8 = (f32[2,2048]{1,0:T(2,128)S(1)}, f32[2,2048]{1,0:T(2,128)}, u32[]{:S(2)}) copy-start(f32[2,2048]{1,0:T(2,128)} %param.21) | copy-start | bytes 49156
  98.4 3.9 %collective-permute-start = (f32[4,4,2,2048]{3,1,0,2:T(4,128)S(1)}, f32[4,4,2,2048]{3,1,0,2:T(4,128)S(1)}, u32[]{:S(2)}, u32[]{:S(2)}) collective-permute-start(f32[4,4,2,2048]{3,1,0,2:T(4,128)S(1)} %dynamic-slice_bitcast_fusion), channel_id=1, source_target_pairs={{0,1},{1,0},{2,3},{3,2},{4,5},{5,4},{6,7},{7,6},{8,9},{9,8},{10,11... | collective-permute-start | bytes 786440 | tf_op jit(solution)/shard_map/ppermute | solution.py:169
  102.3 13.4 %collective-permute-start.3 = (f32[4,4,2,2048]{3,1,0,2:T(4,128)S(1)}, f32[4,4,2,2048]{3,1,0,2:T(4,128)S(1)}, u32[]{:S(2)}, u32[]{:S(2)}) collective-permute-start(f32[4,4,2,2048]{3,1,0,2:T(4,128)S(1)} %bitcast_add_fusion), channel_id=1, source_target_pairs={{0,6},{1,7},{2,0},{3,1},{4,2},{5,3},{6,4},{7,5},{8,14},{9,15},{10,... | collective-permute-start | bytes 786440 | tf_op jit(solution)/shard_map/ppermute | solution.py:174
  104.9 10.8 %collective-permute-start.2 = (f32[4,4,2,2048]{3,1,0,2:T(4,128)S(1)}, f32[4,4,2,2048]{3,1,0,2:T(4,128)S(1)}, u32[]{:S(2)}, u32[]{:S(2)}) collective-permute-start(f32[4,4,2,2048]{3,1,0,2:T(4,128)S(1)} %bitcast_add_fusion), channel_id=1, source_target_pairs={{0,4},{1,5},{2,6},{3,7},{4,0},{5,1},{6,2},{7,3},{8,12},{9,13},{10,... | collective-permute-start | bytes 786440 | tf_op jit(solution)/shard_map/ppermute | solution.py:174
  105.4 14.8 %collective-permute-start.1 = (f32[4,4,2,2048]{3,1,0,2:T(4,128)S(1)}, f32[4,4,2,2048]{3,1,0,2:T(4,128)S(1)}, u32[]{:S(2)}, u32[]{:S(2)}) collective-permute-start(f32[4,4,2,2048]{3,1,0,2:T(4,128)S(1)} %bitcast_add_fusion), channel_id=1, source_target_pairs={{0,2},{1,3},{2,4},{3,5},{4,6},{5,7},{6,0},{7,1},{8,10},{9,11},{10,... | collective-permute-start | bytes 786440 | tf_op jit(solution)/shard_map/ppermute | solution.py:174
  120.9 1.5 collective-permute-start.4
  122.5 6.0 %collective-permute-start.5 = (bf16[32,2048]{1,0:T(8,128)(2,1)S(1)}, bf16[32,2048]{1,0:T(8,128)(2,1)S(1)}, u32[]{:S(2)}, u32[]{:S(2)}) collective-permute-start(bf16[32,2048]{1,0:T(8,128)(2,1)S(1)} %select_n.304), channel_id=1, source_target_pairs={{0,8},{8,16},{16,24},{24,0},{32,40},{40,48},{48,56},{56,32},{64,72... | collective-permute-start | bytes 393224 | tf_op jit(solution)/shard_map/ppermute | solution.py:206
  123.1 8.5 %collective-permute-start.6 = (bf16[32,2048]{1,0:T(8,128)(2,1)S(1)}, bf16[32,2048]{1,0:T(8,128)(2,1)S(1)}, u32[]{:S(2)}, u32[]{:S(2)}) collective-permute-start(bf16[32,2048]{1,0:T(8,128)(2,1)S(1)} %select_n.304), channel_id=1, source_target_pairs={{0,16},{8,24},{16,0},{24,8},{32,48},{40,56},{48,32},{56,40},{64,80... | collective-permute-start | bytes 393224 | tf_op jit(solution)/shard_map/ppermute | solution.py:206
  125.5 6.7 %collective-permute-start.7 = (bf16[32,2048]{1,0:T(8,128)(2,1)S(1)}, bf16[32,2048]{1,0:T(8,128)(2,1)S(1)}, u32[]{:S(2)}, u32[]{:S(2)}) collective-permute-start(bf16[32,2048]{1,0:T(8,128)(2,1)S(1)} %select_n.304), channel_id=1, source_target_pairs={{0,24},{8,0},{16,8},{24,16},{32,56},{40,32},{48,40},{56,48},{64,88... | collective-permute-start | bytes 393224 | tf_op jit(solution)/shard_map/ppermute | solution.py:206
  132.9 13.4 %collective-permute-start.8 = (bf16[128,2048]{1,0:T(8,128)(2,1)S(1)}, bf16[128,2048]{1,0:T(8,128)(2,1)S(1)}, u32[]{:S(2)}, u32[]{:S(2)}) collective-permute-start(bf16[128,2048]{1,0:T(8,128)(2,1)S(1)} %get-tuple-element.19), channel_id=1, source_target_pairs={{0,32},{8,40},{16,48},{24,56},{32,64},{40,72},{48,80},{56,88},{64,... | collective-permute-start | bytes 1572872 | tf_op jit(solution)/shard_map/ppermute | solution.py:212
  135.0 12.2 %collective-permute-start.9 = (bf16[128,2048]{1,0:T(8,128)(2,1)S(1)}, bf16[128,2048]{1,0:T(8,128)(2,1)S(1)}, u32[]{:S(2)}, u32[]{:S(2)}) collective-permute-start(bf16[128,2048]{1,0:T(8,128)(2,1)S(1)} %get-tuple-element.19), channel_id=1, source_target_pairs={{0,224},{8,232},{16,240},{24,248},{32,0},{40,8},{48,16},{56,24},{6... | collective-permute-start | bytes 1572872 | tf_op jit(solution)/shard_map/ppermute | solution.py:215
  146.3 12.5 %collective-permute-start.10 = (bf16[128,2048]{1,0:T(8,128)(2,1)S(1)}, bf16[128,2048]{1,0:T(8,128)(2,1)S(1)}, u32[]{:S(2)}, u32[]{:S(2)}) collective-permute-start(bf16[128,2048]{1,0:T(8,128)(2,1)S(1)} %collective-permute-done.8), channel_id=1, source_target_pairs={{0,32},{8,40},{16,48},{24,56},{32,64},{40,72},{48,80},{56,88},{64,... | collective-permute-start | bytes 1572872 | tf_op jit(solution)/shard_map/ppermute | solution.py:212
  147.2 11.6 %collective-permute-start.11 = (bf16[128,2048]{1,0:T(8,128)(2,1)S(1)}, bf16[128,2048]{1,0:T(8,128)(2,1)S(1)}, u32[]{:S(2)}, u32[]{:S(2)}) collective-permute-start(bf16[128,2048]{1,0:T(8,128)(2,1)S(1)} %collective-permute-done.9), channel_id=1, source_target_pairs={{0,224},{8,232},{16,240},{24,248},{32,0},{40,8},{48,16},{56,24},{6... | collective-permute-start | bytes 1572872 | tf_op jit(solution)/shard_map/ppermute | solution.py:215
  158.9 11.6 %collective-permute-start.12 = (bf16[128,2048]{1,0:T(8,128)(2,1)S(1)}, bf16[128,2048]{1,0:T(8,128)(2,1)S(1)}, u32[]{:S(2)}, u32[]{:S(2)}) collective-permute-start(bf16[128,2048]{1,0:T(8,128)(2,1)S(1)} %collective-permute-done.10), channel_id=1, source_target_pairs={{0,32},{8,40},{16,48},{24,56},{32,64},{40,72},{48,80},{56,88},{64,... | collective-permute-start | bytes 1572872 | tf_op jit(solution)/shard_map/ppermute | solution.py:212
  158.9 11.7 %collective-permute-start.13 = (bf16[128,2048]{1,0:T(8,128)(2,1)S(1)}, bf16[128,2048]{1,0:T(8,128)(2,1)S(1)}, u32[]{:S(2)}, u32[]{:S(2)}) collective-permute-start(bf16[128,2048]{1,0:T(8,128)(2,1)S(1)} %collective-permute-done.11), channel_id=1, source_target_pairs={{0,224},{8,232},{16,240},{24,248},{32,0},{40,8},{48,16},{56,24},{6... | collective-permute-start | bytes 1572872 | tf_op jit(solution)/shard_map/ppermute | solution.py:215
  162.4 21.2 %copy-start.11 = (s32[8]{0:T(128)S(1)}, s32[8]{0:T(128)}, u32[]{:S(2)}) copy-start(s32[8]{0:T(128)} %constant.215) | copy-start | bytes 100
  162.4 21.3 %copy-start.10 = (s32[1024]{0:T(1024)S(1)}, s32[1024]{0:T(1024)}, u32[]{:S(2)}) copy-start(s32[1024]{0:T(1024)} %param.24) | copy-start | bytes 12292
  170.5 6.5 %collective-permute-start.14 = (bf16[64,2048]{1,0:T(8,128)(2,1)S(1)}, bf16[64,2048]{1,0:T(8,128)(2,1)S(1)}, u32[]{:S(2)}, u32[]{:S(2)}) collective-permute-start(bf16[64,2048]{1,0:T(8,128)(2,1)S(1)} %slice.103), channel_id=1, source_target_pairs={{0,32},{8,40},{16,48},{24,56},{32,64},{40,72},{48,80},{56,88},{64,... | collective-permute-start | bytes 786440 | tf_op jit(solution)/shard_map/ppermute | solution.py:220
  170.6 7.1 %collective-permute-start.15 = (bf16[64,2048]{1,0:T(8,128)(2,1)S(1)}, bf16[64,2048]{1,0:T(8,128)(2,1)S(1)}, u32[]{:S(2)}, u32[]{:S(2)}) collective-permute-start(bf16[64,2048]{1,0:T(8,128)(2,1)S(1)} %slice.104), channel_id=1, source_target_pairs={{0,224},{8,232},{16,240},{24,248},{32,0},{40,8},{48,16},{56,24},{6... | collective-permute-start | bytes 786440 | tf_op jit(solution)/shard_map/ppermute | solution.py:221
  178.4 15.5 %collective-permute-start.16 = (bf16[1024,2048]{1,0:T(8,128)(2,1)}, bf16[1024,2048]{1,0:T(8,128)(2,1)}, u32[]{:S(2)}, u32[]{:S(2)}) collective-permute-start(bf16[1024,2048]{1,0:T(8,128)(2,1)} %constant_dynamic-update-slice_fusion.4), channel_id=1, source_target_pairs={{0,1},{1,0},{2,3},{3,2},{4,5},{5,4},{6,7},{7,6},{8,9},{9,8},{10,11... | collective-permute-start | bytes 12582920 | tf_op jit(solution)/shard_map/ppermute | solution.py:225
  202.3 9.9 %copy-start.1 = (s32[2]{0:T(128)S(1)}, s32[2]{0:T(128)}, u32[]{:S(2)}) copy-start(s32[2]{0:T(128)} %param.18) | copy-start | bytes 28
  208.9 8.0 %all-to-all-start.1 = ((f32[8,1,768]{2,1,0:T(1,128)}), f32[8,1,768]{2,1,0:T(1,128)S(1)}, u32[]{:S(2)}, u32[]{:S(2)}) async-start(f32[8,1,768]{2,1,0:T(1,128)} %reshape.703), calls=%async_computation.1 | async-start | bytes 49152 | tf_op jit(solution)/shard_map/all_to_all | solution.py:254
  219.0 17.2 %all-to-all-start.2 = ((f32[3,2,32,4]{3,1,0,2:T(2,128)}), f32[3,2,32,4]{3,1,0,2:T(2,128)S(1)}, u32[]{:S(2)}, u32[]{:S(2)}) async-start(f32[3,2,32,4]{3,1,0,2:T(2,128)} %copy.78), calls=%async_computation.2 | async-start | bytes 196608 | tf_op jit(solution)/shard_map/all_to_all | solution.py:256
where the time goes:
time: 237 us
  waiting for transfers between devices  123 us (52%)
  starting transfers between devices  50.6 us (21%)
  local copies, waits for them, and re-layouts  24.7 us (10%)
  matrix products  22.7 us (10%)
  other arithmetic  15.5 us (7%)
    all_to_all x1, waiting for transfers between devices, per_device(): lax.all_to_all(outgoing.reshape(buffer, -1, flat_width), 'group', split_a...  61.7 us
    ppermute x3, waiting for transfers between devices, per_device(): forward = lax.ppermute(forward, 'group', z_shift(1))  26.1 us
    dot_general x2, matrix products, local_stats(): logits = jnp.dot(rows, weights, preferred_element_type=jnp.float32)  16.7 us
    ppermute x3, waiting for transfers between devices, per_device(): hidden = hidden + lax.ppermute(pair_sum, 'tensor', x_shift(k))  14.2 us
    all_to_all x1, starting transfers between devices, per_device(): lax.all_to_all(outgoing.reshape(buffer, -1, flat_width), 'group', split_a...  12.3 us
    unnamed x40, local copies, waits for them, and re-layouts  9.5 us
    all_to_all x1, waiting for transfers between devices, per_device(): lax.all_to_all(jnp.stack([peak, total, chosen]), 'group', 2, 2, tiled=True)  9.06 us
    all_to_all x1, starting transfers between devices, per_device(): lax.all_to_all(jnp.stack([peak, total, chosen]), 'group', 2, 2, tiled=True)  8.09 us
  transfers between devices with their start and end apart: 20, of which 13 were waited for; matrix products, arithmetic and copies ran while one was open for 12% of the time, Pallas kernels for 0%

commit v1 on v0

--- a/solution.py
+++ b/solution.py
@@ -154,9 +154,6 @@
     x_id = tensor_id // 2
     swap = [(t, t ^ 1) for t in range(shards)]
 
-    def x_shift(step):
-        return [(t, (t + 2 * step) % shards) for t in range(shards)]
-
     partial = jnp.einsum("mtk,mkd->tmd", attended, out_proj, preferred_element_type=jnp.float32)
     partial = partial.reshape(x_size, 2, rows_local, 2, width)
     own_rows = jnp.transpose(residual.astype(jnp.float32), (1, 0, 2))
@@ -170,8 +167,10 @@
         lax.dynamic_index_in_dim(partial, 1 - side, 1, keepdims=False), "tensor", swap
     )
     hidden = pair_sum
-    for k in range(1, x_size):
-        hidden = hidden + lax.ppermute(pair_sum, "tensor", x_shift(k))
+    step = 2
+    while step < shards:
+        hidden = hidden + lax.ppermute(hidden, "tensor", [(t, t ^ step) for t in range(shards)])
+        step *= 2
     hidden = jnp.transpose(hidden.reshape(x_size * rows_local, 2, width), (1, 0, 2))
     row_mean = jnp.mean(hidden, axis=-1, keepdims=True)
     centered = hidden - row_mean

time: 237 us -> 238 us (level)
  starting transfers between devices: 50.6 us -> 54 us
  waiting for transfers between devices: 123 us -> 120 us
    ppermute x3 -> x2, waiting for transfers between devices: 14.2 us -> 11.7 us  [per_device(): lax.ppermute(hidden, 'tensor', [(t, t ^ step) for t in range(shards)])]
  transfers between devices with their start and end apart: 20 -> 19, of which waited for: 13 -> 13; matrix products, arithmetic and copies ran while one was open for 12% -> 12% of each run, Pallas kernels for 0% -> 0%
where the time goes in v1:
time: 238 us
  waiting for transfers between devices  120 us (50%)
  starting transfers between devices  54 us (23%)
  local copies, waits for them, and re-layouts  24.7 us (10%)
  matrix products  22.7 us (10%)
  other arithmetic  15.6 us (7%)
    all_to_all x1, waiting for transfers between devices, per_device(): lax.all_to_all(outgoing.reshape(buffer, -1, flat_width), 'group', split_a...  61.7 us
    ppermute x3, waiting for transfers between devices, per_device(): forward = lax.ppermute(forward, 'group', z_shift(1))  26.1 us
    dot_general x2, matrix products, local_stats(): logits = jnp.dot(rows, weights, preferred_element_type=jnp.float32)  16.7 us
    all_to_all x1, starting transfers between devices, per_device(): lax.all_to_all(outgoing.reshape(buffer, -1, flat_width), 'group', split_a...  12.3 us
    ppermute x2, waiting for transfers between devices, per_device(): lax.ppermute(hidden, 'tensor', [(t, t ^ step) for t in range(shards)])  11.7 us
    unnamed x40, local copies, waits for them, and re-layouts  9.5 us
    all_to_all x1, waiting for transfers between devices, per_device(): lax.all_to_all(jnp.stack([peak, total, chosen]), 'group', 2, 2, tiled=True)  9.06 us
    all_to_all x1, starting transfers between devices, per_device(): lax.all_to_all(jnp.stack([peak, total, chosen]), 'group', 2, 2, tiled=True)  8.09 us
  transfers between devices with their start and end apart: 19, of which 13 were waited for; matrix products, arithmetic and copies ran while one was open for 12% of the time, Pallas kernels for 0%

profile of v1, /device:TPU:1, one launch (start us, length us, event | category | flops | bytes accessed | tf_op | source)
XLA Modules:
  0.0 237.9 jit_solution(3387646348296671713)
XLA Ops:
  0.0 0.9 fusion.84
  1.1 0.8 multiply_add_fusion
  1.8 2.8 %convert_bitcast_fusion = bf16[96,2,2,16,256]{4,0,1,3,2:T(8,128)(2,1)S(1)} fusion(bf16[2,48,16,2,256]{4,3,2,1,0:T(2,128)(2,1)} %param.15, s32[48]{0:T(128)S(1)} %multiply_add_fusion), kind=kOutput, calls=%fused_computation.15 | convolution fusion | flops 152572416 | bytes 4718784 | tf_op jit(solution)/shard_map/sp,mpjcx->scmjx/dot_general | solution.py:66
  4.6 3.5 %copy.64 = bf16[96,2,2,16,256]{4,3,2,1,0:T(8,128)(2,1)} copy(bf16[96,2,2,16,256]{4,0,1,3,2:T(8,128)(2,1)S(1)} %convert_bitcast_fusion) | data formatting | bytes 6291456 | tf_op jit(solution)/shard_map/convert_element_type | solution.py:68
  8.1 12.3 %all-to-all-start = ((bf16[96,64,256]{2,1,0:T(8,128)(2,1)}), bf16[96,64,256]{2,1,0:T(8,128)(2,1)}, u32[]{:S(2)}, u32[]{:S(2)}) async-start(bf16[96,64,256]{2,1,0:T(8,128)(2,1)} %bitcast.157), calls=%async_computation | async-start | bytes 6291456 | tf_op jit(solution)/shard_map/all_to_all | solution.py:69
  20.6 0.6 convert_reduce_fusion
  21.5 0.6 fusion.97
  22.1 1.2 fusion.81
  23.3 0.6 fusion.96
  24.8 1.4 convert_multiply_fusion.3
  26.8 2.4 %convert_multiply_fusion.1 = (f32[32,96,16]{0,2,1:T(8,128)}, f32[32,96,16]{0,2,1:T(8,128)S(1)}) fusion(s32[96,16]{1,0:T(8,128)S(1)} %iota_add_fusion, s32[32]{0:T(128)S(1)} %fusion.81, f32[]{:T(128)} %bitcast.12, f32[]{:T(128)} %bitcast.24), kind=kLoop, calls=%fused_computation.53 | loop fusion | flops 196608 | bytes 399496 | tf_op jit(solution)/shard_map/mul | solution.py:133
  29.3 61.7 %all-to-all-done = bf16[96,64,256]{2,1,0:T(8,128)(2,1)} async-done(((bf16[96,64,256]{2,1,0:T(8,128)(2,1)}), bf16[96,64,256]{2,1,0:T(8,128)(2,1)}, u32[]{:S(2)}, u32[]{:S(2)}) %all-to-all-start) | async-done | bytes 3145760 | tf_op jit(solution)/shard_map/all_to_all | solution.py:69
  91.0 2.2 fusion.94
  93.5 0.8 copy-done.2
  95.9 0.7 fusion.9
  98.4 2.7 %collective-permute-start = (f32[4,4,2,2048]{3,1,0,2:T(4,128)S(1)}, f32[4,4,2,2048]{3,1,0,2:T(4,128)S(1)}, u32[]{:S(2)}, u32[]{:S(2)}) collective-permute-start(f32[4,4,2,2048]{3,1,0,2:T(4,128)S(1)} %dynamic-slice_bitcast_fusion), channel_id=1, source_target_pairs={{0,1},{1,0},{2,3},{3,2},{4,5},{5,4},{6,7},{7,6},{8,9},{9,8},{10,11... | collective-permute-start | bytes 786440 | tf_op jit(solution)/shard_map/ppermute | solution.py:166
  101.1 1.2 collective-permute-done
  102.3 1.3 collective-permute-start.1
  103.6 6.3 %collective-permute-done.1 = f32[4,4,2,2048]{3,1,0,2:T(4,128)S(1)} collective-permute-done((f32[4,4,2,2048]{3,1,0,2:T(4,128)S(1)}, f32[4,4,2,2048]{3,1,0,2:T(4,128)S(1)}, u32[]{:S(2)}, u32[]{:S(2)}) %collective-permute-start.1) | collective-permute-done | bytes 262176 | tf_op jit(solution)/shard_map/ppermute | solution.py:172
  110.0 2.8 %collective-permute-start.2 = (f32[4,4,2,2048]{3,1,0,2:T(4,128)S(1)}, f32[4,4,2,2048]{3,1,0,2:T(4,128)S(1)}, u32[]{:S(2)}, u32[]{:S(2)}) collective-permute-start(f32[4,4,2,2048]{3,1,0,2:T(4,128)S(1)} %add.341), channel_id=1, source_target_pairs={{0,4},{1,5},{2,6},{3,7},{4,0},{5,1},{6,2},{7,3},{8,12},{9,13},{10,... | collective-permute-start | bytes 786440 | tf_op jit(solution)/shard_map/ppermute | solution.py:172
  112.9 5.4 %collective-permute-done.2 = f32[4,4,2,2048]{3,1,0,2:T(4,128)S(1)} collective-permute-done((f32[4,4,2,2048]{3,1,0,2:T(4,128)S(1)}, f32[4,4,2,2048]{3,1,0,2:T(4,128)S(1)}, u32[]{:S(2)}, u32[]{:S(2)}) %collective-permute-start.2) | collective-permute-done | bytes 262176 | tf_op jit(solution)/shard_map/ppermute | solution.py:172
  118.9 2.4 %collective-permute-start.3 = (bf16[16,2048]{1,0:T(8,128)(2,1)S(1)}, bf16[16,2048]{1,0:T(8,128)(2,1)S(1)}, u32[]{:S(2)}, u32[]{:S(2)}) collective-permute-start(bf16[16,2048]{1,0:T(8,128)(2,1)S(1)} %get-tuple-element.28), channel_id=1, source_target_pairs={{0,1},{1,0},{2,3},{3,2},{4,5},{5,4},{6,7},{7,6},{8,9},{9,8},{10,11... | collective-permute-start | bytes 196616 | tf_op jit(solution)/shard_map/ppermute | solution.py:189
  121.3 0.9 collective-permute-done.3
  122.9 2.4 %collective-permute-start.5 = (bf16[32,2048]{1,0:T(8,128)(2,1)S(1)}, bf16[32,2048]{1,0:T(8,128)(2,1)S(1)}, u32[]{:S(2)}, u32[]{:S(2)}) collective-permute-start(bf16[32,2048]{1,0:T(8,128)(2,1)S(1)} %select_n.304), channel_id=1, source_target_pairs={{0,16},{8,24},{16,0},{24,8},{32,48},{40,56},{48,32},{56,40},{64,80... | collective-permute-start | bytes 393224 | tf_op jit(solution)/shard_map/ppermute | solution.py:205
  125.3 1.1 collective-permute-start.6
  126.3 0.7 constant_dynamic-update-slice_fusion.3
  127.0 1.4 collective-permute-done.4
  128.3 0.7 constant_dynamic-update-slice_fusion.2
  129.0 2.3 collective-permute-done.5
  131.3 0.7 constant_dynamic-update-slice_fusion.1
  132.0 0.7 constant_dynamic-update-slice_fusion
  132.7 2.1 collective-permute-start.7
  134.8 0.6 collective-permute-start.8
  135.4 10.8 %collective-permute-done.7 = bf16[128,2048]{1,0:T(8,128)(2,1)S(1)} collective-permute-done((bf16[128,2048]{1,0:T(8,128)(2,1)S(1)}, bf16[128,2048]{1,0:T(8,128)(2,1)S(1)}, u32[]{:S(2)}, u32[]{:S(2)}) %collective-permute-start.7) | collective-permute-done | bytes 524320 | tf_op jit(solution)/shard_map/ppermute | solution.py:211
  146.1 0.9 collective-permute-start.9
  147.0 1.8 collective-permute-start.10
  148.8 0.9 constant_dynamic-update-slice_fusion.11
  149.7 9.0 %collective-permute-done.9 = bf16[128,2048]{1,0:T(8,128)(2,1)S(1)} collective-permute-done((bf16[128,2048]{1,0:T(8,128)(2,1)S(1)}, bf16[128,2048]{1,0:T(8,128)(2,1)S(1)}, u32[]{:S(2)}, u32[]{:S(2)}) %collective-permute-start.9) | collective-permute-done | bytes 524320 | tf_op jit(solution)/shard_map/ppermute | solution.py:211
  158.6 2.7 %collective-permute-start.12 = (bf16[128,2048]{1,0:T(8,128)(2,1)S(1)}, bf16[128,2048]{1,0:T(8,128)(2,1)S(1)}, u32[]{:S(2)}, u32[]{:S(2)}) collective-permute-start(bf16[128,2048]{1,0:T(8,128)(2,1)S(1)} %collective-permute-done.10), channel_id=1, source_target_pairs={{0,224},{8,232},{16,240},{24,248},{32,0},{40,8},{48,16},{56,24},{6... | collective-permute-start | bytes 1572872 | tf_op jit(solution)/shard_map/ppermute | solution.py:214
  161.3 0.8 constant_dynamic-update-slice_fusion.10
  162.2 0.8 constant_dynamic-update-slice_fusion.9
  163.0 0.8 constant_dynamic-update-slice_fusion.8
  163.9 6.4 %collective-permute-done.11 = bf16[128,2048]{1,0:T(8,128)(2,1)S(1)} collective-permute-done((bf16[128,2048]{1,0:T(8,128)(2,1)S(1)}, bf16[128,2048]{1,0:T(8,128)(2,1)S(1)}, u32[]{:S(2)}, u32[]{:S(2)}) %collective-permute-start.11) | collective-permute-done | bytes 524320 | tf_op jit(solution)/shard_map/ppermute | solution.py:211
  170.4 2.7 %collective-permute-start.14 = (bf16[64,2048]{1,0:T(8,128)(2,1)S(1)}, bf16[64,2048]{1,0:T(8,128)(2,1)S(1)}, u32[]{:S(2)}, u32[]{:S(2)}) collective-permute-start(bf16[64,2048]{1,0:T(8,128)(2,1)S(1)} %slice.104), channel_id=1, source_target_pairs={{0,224},{8,232},{16,240},{24,248},{32,0},{40,8},{48,16},{56,24},{6... | collective-permute-start | bytes 786440 | tf_op jit(solution)/shard_map/ppermute | solution.py:220
  173.1 0.9 constant_dynamic-update-slice_fusion.7
  174.0 0.8 constant_dynamic-update-slice_fusion.6
  174.8 2.0 collective-permute-done.13
  176.8 0.7 constant_dynamic-update-slice_fusion.5
  177.5 0.7 constant_dynamic-update-slice_fusion.4
  178.2 5.1 %collective-permute-start.15 = (bf16[1024,2048]{1,0:T(8,128)(2,1)}, bf16[1024,2048]{1,0:T(8,128)(2,1)}, u32[]{:S(2)}, u32[]{:S(2)}) collective-permute-start(bf16[1024,2048]{1,0:T(8,128)(2,1)} %constant_dynamic-update-slice_fusion.4), channel_id=1, source_target_pairs={{0,1},{1,0},{2,3},{3,2},{4,5},{5,4},{6,7},{7,6},{8,9},{9,8},{10,11... | collective-permute-start | bytes 12582920 | tf_op jit(solution)/shard_map/ppermute | solution.py:224
  183.6 0.9 scatter_custom_fusion
  185.2 8.4 %fusion.103 = (f32[1024]{0:T(1024)S(1)}, f32[1024,768]{0,1:T(8,128)}) fusion(bf16[1024,2048]{1,0:T(8,128)(2,1)} %constant_dynamic-update-slice_fusion.4, bf16[2,2048,768]{2,1,0:T(8,128)(2,1)} %param.23, s32[]{:T(128)S(6)} %select_n.301), kind=kOutput, calls=%fused_computation.234 | convolution fusion | flops 3222010880 | bytes 10489860 | tf_op jit(solution)/shard_map/dot_general | solution.py:234
  193.7 8.3 %fusion.102 = (f32[1024]{0:T(1024)S(1)}, f32[1024,768]{0,1:T(8,128)}) fusion(bf16[1024,2048]{1,0:T(8,128)(2,1)} %collective-permute-done.15, bf16[2,2048,768]{2,1,0:T(8,128)(2,1)} %param.23, s32[]{:T(128)S(6)} %select_n.302), kind=kOutput, calls=%fused_computation.233 | convolution fusion | flops 3222010880 | bytes 10489860 | tf_op jit(solution)/shard_map/dot_general | solution.py:234
  202.1 4.4 %select_reduce_fusion.1 = (f32[1024]{0:T(1024)S(1)}, f32[1024]{0:T(1024)S(1)}, f32[1024]{0:T(1024)S(1)}, f32[1024]{0:T(1024)S(1)}) fusion(f32[1024,768]{0,1:T(8,128)} %get-tuple-element.52, s32[1024]{0:T(1024)S(1)} %sub.261, f32[1024]{0:T(1024)S(1)} %get-tuple-element.51, f32[1024,768]{0,1:T(8,128)} %get-tuple-element.50, f32[1024]{0:T(1024)S(1)} %get-tuple-element.49), kind=kLoop, calls=%fused_computation.11 | loop fusion | flops 7073792 | bytes 6320128 | tf_op jit(solution)/shard_map/reduce_sum | solution.py:237
  207.1 0.7 gather_fusion.2
  208.0 0.7 reshape.703
  208.7 4.4 %all-to-all-start.1 = ((f32[8,1,768]{2,1,0:T(1,128)}), f32[8,1,768]{2,1,0:T(1,128)S(1)}, u32[]{:S(2)}, u32[]{:S(2)}) async-start(f32[8,1,768]{2,1,0:T(1,128)} %reshape.703), calls=%async_computation.1 | async-start | bytes 49152 | tf_op jit(solution)/shard_map/all_to_all | solution.py:253
  213.1 0.6 gather_fusion
  213.8 4.0 %all-to-all-done.1 = f32[8,1,768]{2,1,0:T(1,128)S(1)} async-done(((f32[8,1,768]{2,1,0:T(1,128)}), f32[8,1,768]{2,1,0:T(1,128)S(1)}, u32[]{:S(2)}, u32[]{:S(2)}) %all-to-all-start.1) | async-done | bytes 24608 | tf_op jit(solution)/shard_map/all_to_all | solution.py:253
  218.3 0.7 reduce.11
  219.2 0.7 copy.78
  220.0 8.1 %all-to-all-start.2 = ((f32[3,2,32,4]{3,1,0,2:T(2,128)}), f32[3,2,32,4]{3,1,0,2:T(2,128)S(1)}, u32[]{:S(2)}, u32[]{:S(2)}) async-start(f32[3,2,32,4]{3,1,0,2:T(2,128)} %copy.78), calls=%async_computation.2 | async-start | bytes 196608 | tf_op jit(solution)/shard_map/all_to_all | solution.py:255
  228.1 9.1 %all-to-all-done.2 = f32[3,2,32,4]{3,1,0,2:T(2,128)S(1)} async-done(((f32[3,2,32,4]{3,1,0,2:T(2,128)}), f32[3,2,32,4]{3,1,0,2:T(2,128)S(1)}, u32[]{:S(2)}, u32[]{:S(2)}) %all-to-all-start.2) | async-done | bytes 3104 | tf_op jit(solution)/shard_map/all_to_all | solution.py:255
  237.3 0.6 subtract_select_fusion
  (126 shorter events, 10.0 us)
Async XLA Ops:
  0.0 97.6 %copy-start = (bf16[2,256,2048]{2,1,0:T(8,128)(2,1)S(1)}, bf16[2,256,2048]{2,1,0:T(8,128)(2,1)}, u32[]{:S(2)}) copy-start(bf16[2,256,2048]{2,1,0:T(8,128)(2,1)} %param.19) | copy-start | bytes 6291460
  8.1 12.3 %copy-start.9 = (s32[1536,1]{0,1:T(1,128)S(1)}, s32[1536,1]{0,1:T(1,128)}, u32[]{:S(2)}) copy-start(s32[1536,1]{0,1:T(1,128)} %param.16) | copy-start | bytes 18436
  8.1 13.3 %copy-start.4 = (s32[1536]{0:T(1024)S(1)}, s32[1536]{0:T(1024)}, u32[]{:S(2)}) copy-start(s32[1536]{0:T(1024)} %param.17) | copy-start | bytes 18436
  8.1 18.1 %copy-start.3 = (bf16[2,32,2,256]{3,2,1,0:T(2,128)(2,1)S(1)}, bf16[2,32,2,256]{3,2,1,0:T(2,128)(2,1)}, u32[]{:S(2)}) copy-start(bf16[2,32,2,256]{3,2,1,0:T(2,128)(2,1)} %param.14) | copy-start | bytes 196612
  8.1 18.3 %copy-start.6 = (bf16[2,32,256]{2,1,0:T(8,128)(2,1)S(1)}, bf16[2,32,256]{2,1,0:T(8,128)(2,1)}, u32[]{:S(2)}) copy-start(bf16[2,32,256]{2,1,0:T(8,128)(2,1)} %param.13) | copy-start | bytes 98308
  8.1 82.9 %all-to-all-start = ((bf16[96,64,256]{2,1,0:T(8,128)(2,1)}), bf16[96,64,256]{2,1,0:T(8,128)(2,1)}, u32[]{:S(2)}, u32[]{:S(2)}) async-start(bf16[96,64,256]{2,1,0:T(8,128)(2,1)} %bitcast.157), calls=%async_computation | async-start | bytes 6291456 | tf_op jit(solution)/shard_map/all_to_all | solution.py:69
  93.2 1.1 copy-start.2
  96.6 1.7 copy-start.5
  98.1 20.6 %copy-start.7 = (f32[2,2048]{1,0:T(2,128)S(1)}, f32[2,2048]{1,0:T(2,128)}, u32[]{:S(2)}) copy-start(f32[2,2048]{1,0:T(2,128)} %param.22) | copy-start | bytes 49156
  98.1 20.6 %copy-start.8 = (f32[2,2048]{1,0:T(2,128)S(1)}, f32[2,2048]{1,0:T(2,128)}, u32[]{:S(2)}) copy-start(f32[2,2048]{1,0:T(2,128)} %param.21) | copy-start | bytes 49156
  98.4 3.9 %collective-permute-start = (f32[4,4,2,2048]{3,1,0,2:T(4,128)S(1)}, f32[4,4,2,2048]{3,1,0,2:T(4,128)S(1)}, u32[]{:S(2)}, u32[]{:S(2)}) collective-permute-start(f32[4,4,2,2048]{3,1,0,2:T(4,128)S(1)} %dynamic-slice_bitcast_fusion), channel_id=1, source_target_pairs={{0,1},{1,0},{2,3},{3,2},{4,5},{5,4},{6,7},{7,6},{8,9},{9,8},{10,11... | collective-permute-start | bytes 786440 | tf_op jit(solution)/shard_map/ppermute | solution.py:166
  102.3 7.6 %collective-permute-start.1 = (f32[4,4,2,2048]{3,1,0,2:T(4,128)S(1)}, f32[4,4,2,2048]{3,1,0,2:T(4,128)S(1)}, u32[]{:S(2)}, u32[]{:S(2)}) collective-permute-start(f32[4,4,2,2048]{3,1,0,2:T(4,128)S(1)} %bitcast_add_fusion), channel_id=1, source_target_pairs={{0,2},{1,3},{2,0},{3,1},{4,6},{5,7},{6,4},{7,5},{8,10},{9,11},{10,... | collective-permute-start | bytes 786440 | tf_op jit(solution)/shard_map/ppermute | solution.py:172
  110.0 8.2 %collective-permute-start.2 = (f32[4,4,2,2048]{3,1,0,2:T(4,128)S(1)}, f32[4,4,2,2048]{3,1,0,2:T(4,128)S(1)}, u32[]{:S(2)}, u32[]{:S(2)}) collective-permute-start(f32[4,4,2,2048]{3,1,0,2:T(4,128)S(1)} %add.341), channel_id=1, source_target_pairs={{0,4},{1,5},{2,6},{3,7},{4,0},{5,1},{6,2},{7,3},{8,12},{9,13},{10,... | collective-permute-start | bytes 786440 | tf_op jit(solution)/shard_map/ppermute | solution.py:172
  118.9 3.3 %collective-permute-start.3 = (bf16[16,2048]{1,0:T(8,128)(2,1)S(1)}, bf16[16,2048]{1,0:T(8,128)(2,1)S(1)}, u32[]{:S(2)}, u32[]{:S(2)}) collective-permute-start(bf16[16,2048]{1,0:T(8,128)(2,1)S(1)} %get-tuple-element.28), channel_id=1, source_target_pairs={{0,1},{1,0},{2,3},{3,2},{4,5},{5,4},{6,7},{7,6},{8,9},{9,8},{10,11... | collective-permute-start | bytes 196616 | tf_op jit(solution)/shard_map/ppermute | solution.py:189
  122.3 6.0 %collective-permute-start.4 = (bf16[32,2048]{1,0:T(8,128)(2,1)S(1)}, bf16[32,2048]{1,0:T(8,128)(2,1)S(1)}, u32[]{:S(2)}, u32[]{:S(2)}) collective-permute-start(bf16[32,2048]{1,0:T(8,128)(2,1)S(1)} %select_n.304), channel_id=1, source_target_pairs={{0,8},{8,16},{16,24},{24,0},{32,40},{40,48},{48,56},{56,32},{64,72... | collective-permute-start | bytes 393224 | tf_op jit(solution)/shard_map/ppermute | solution.py:205
  122.9 8.5 %collective-permute-start.5 = (bf16[32,2048]{1,0:T(8,128)(2,1)S(1)}, bf16[32,2048]{1,0:T(8,128)(2,1)S(1)}, u32[]{:S(2)}, u32[]{:S(2)}) collective-permute-start(bf16[32,2048]{1,0:T(8,128)(2,1)S(1)} %select_n.304), channel_id=1, source_target_pairs={{0,16},{8,24},{16,0},{24,8},{32,48},{40,56},{48,32},{56,40},{64,80... | collective-permute-start | bytes 393224 | tf_op jit(solution)/shard_map/ppermute | solution.py:205
  125.3 6.7 %collective-permute-start.6 = (bf16[32,2048]{1,0:T(8,128)(2,1)S(1)}, bf16[32,2048]{1,0:T(8,128)(2,1)S(1)}, u32[]{:S(2)}, u32[]{:S(2)}) collective-permute-start(bf16[32,2048]{1,0:T(8,128)(2,1)S(1)} %select_n.304), channel_id=1, source_target_pairs={{0,24},{8,0},{16,8},{24,16},{32,56},{40,32},{48,40},{56,48},{64,88... | collective-permute-start | bytes 393224 | tf_op jit(solution)/shard_map/ppermute | solution.py:205
  132.7 13.4 %collective-permute-start.7 = (bf16[128,2048]{1,0:T(8,128)(2,1)S(1)}, bf16[128,2048]{1,0:T(8,128)(2,1)S(1)}, u32[]{:S(2)}, u32[]{:S(2)}) collective-permute-start(bf16[128,2048]{1,0:T(8,128)(2,1)S(1)} %get-tuple-element.19), channel_id=1, source_target_pairs={{0,32},{8,40},{16,48},{24,56},{32,64},{40,72},{48,80},{56,88},{64,... | collective-permute-start | bytes 1572872 | tf_op jit(solution)/shard_map/ppermute | solution.py:211
  134.8 12.2 %collective-permute-start.8 = (bf16[128,2048]{1,0:T(8,128)(2,1)S(1)}, bf16[128,2048]{1,0:T(8,128)(2,1)S(1)}, u32[]{:S(2)}, u32[]{:S(2)}) collective-permute-start(bf16[128,2048]{1,0:T(8,128)(2,1)S(1)} %get-tuple-element.19), channel_id=1, source_target_pairs={{0,224},{8,232},{16,240},{24,248},{32,0},{40,8},{48,16},{56,24},{6... | collective-permute-start | bytes 1572872 | tf_op jit(solution)/shard_map/ppermute | solution.py:214
  146.1 12.5 %collective-permute-start.9 = (bf16[128,2048]{1,0:T(8,128)(2,1)S(1)}, bf16[128,2048]{1,0:T(8,128)(2,1)S(1)}, u32[]{:S(2)}, u32[]{:S(2)}) collective-permute-start(bf16[128,2048]{1,0:T(8,128)(2,1)S(1)} %collective-permute-done.7), channel_id=1, source_target_pairs={{0,32},{8,40},{16,48},{24,56},{32,64},{40,72},{48,80},{56,88},{64,... | collective-permute-start | bytes 1572872 | tf_op jit(solution)/shard_map/ppermute | solution.py:211
  147.0 11.6 %collective-permute-start.10 = (bf16[128,2048]{1,0:T(8,128)(2,1)S(1)}, bf16[128,2048]{1,0:T(8,128)(2,1)S(1)}, u32[]{:S(2)}, u32[]{:S(2)}) collective-permute-start(bf16[128,2048]{1,0:T(8,128)(2,1)S(1)} %collective-permute-done.8), channel_id=1, source_target_pairs={{0,224},{8,232},{16,240},{24,248},{32,0},{40,8},{48,16},{56,24},{6... | collective-permute-start | bytes 1572872 | tf_op jit(solution)/shard_map/ppermute | solution.py:214
  158.6 11.6 %collective-permute-start.11 = (bf16[128,2048]{1,0:T(8,128)(2,1)S(1)}, bf16[128,2048]{1,0:T(8,128)(2,1)S(1)}, u32[]{:S(2)}, u32[]{:S(2)}) collective-permute-start(bf16[128,2048]{1,0:T(8,128)(2,1)S(1)} %collective-permute-done.9), channel_id=1, source_target_pairs={{0,32},{8,40},{16,48},{24,56},{32,64},{40,72},{48,80},{56,88},{64,... | collective-permute-start | bytes 1572872 | tf_op jit(solution)/shard_map/ppermute | solution.py:211
  158.6 11.7 %collective-permute-start.12 = (bf16[128,2048]{1,0:T(8,128)(2,1)S(1)}, bf16[128,2048]{1,0:T(8,128)(2,1)S(1)}, u32[]{:S(2)}, u32[]{:S(2)}) collective-permute-start(bf16[128,2048]{1,0:T(8,128)(2,1)S(1)} %collective-permute-done.10), channel_id=1, source_target_pairs={{0,224},{8,232},{16,240},{24,248},{32,0},{40,8},{48,16},{56,24},{6... | collective-permute-start | bytes 1572872 | tf_op jit(solution)/shard_map/ppermute | solution.py:214
  162.2 21.2 %copy-start.11 = (s32[8]{0:T(128)S(1)}, s32[8]{0:T(128)}, u32[]{:S(2)}) copy-start(s32[8]{0:T(128)} %constant.215) | copy-start | bytes 100
  162.2 21.3 %copy-start.10 = (s32[1024]{0:T(1024)S(1)}, s32[1024]{0:T(1024)}, u32[]{:S(2)}) copy-start(s32[1024]{0:T(1024)} %param.24) | copy-start | bytes 12292
  170.3 6.5 %collective-permute-start.13 = (bf16[64,2048]{1,0:T(8,128)(2,1)S(1)}, bf16[64,2048]{1,0:T(8,128)(2,1)S(1)}, u32[]{:S(2)}, u32[]{:S(2)}) collective-permute-start(bf16[64,2048]{1,0:T(8,128)(2,1)S(1)} %slice.103), channel_id=1, source_target_pairs={{0,32},{8,40},{16,48},{24,56},{32,64},{40,72},{48,80},{56,88},{64,... | collective-permute-start | bytes 786440 | tf_op jit(solution)/shard_map/ppermute | solution.py:219
  170.4 7.1 %collective-permute-start.14 = (bf16[64,2048]{1,0:T(8,128)(2,1)S(1)}, bf16[64,2048]{1,0:T(8,128)(2,1)S(1)}, u32[]{:S(2)}, u32[]{:S(2)}) collective-permute-start(bf16[64,2048]{1,0:T(8,128)(2,1)S(1)} %slice.104), channel_id=1, source_target_pairs={{0,224},{8,232},{16,240},{24,248},{32,0},{40,8},{48,16},{56,24},{6... | collective-permute-start | bytes 786440 | tf_op jit(solution)/shard_map/ppermute | solution.py:220
  178.2 15.5 %collective-permute-start.15 = (bf16[1024,2048]{1,0:T(8,128)(2,1)}, bf16[1024,2048]{1,0:T(8,128)(2,1)}, u32[]{:S(2)}, u32[]{:S(2)}) collective-permute-start(bf16[1024,2048]{1,0:T(8,128)(2,1)} %constant_dynamic-update-slice_fusion.4), channel_id=1, source_target_pairs={{0,1},{1,0},{2,3},{3,2},{4,5},{5,4},{6,7},{7,6},{8,9},{9,8},{10,11... | collective-permute-start | bytes 12582920 | tf_op jit(solution)/shard_map/ppermute | solution.py:224
  202.1 11.0 %copy-start.1 = (s32[2]{0:T(128)S(1)}, s32[2]{0:T(128)}, u32[]{:S(2)}) copy-start(s32[2]{0:T(128)} %param.18) | copy-start | bytes 28
  208.7 9.1 %all-to-all-start.1 = ((f32[8,1,768]{2,1,0:T(1,128)}), f32[8,1,768]{2,1,0:T(1,128)S(1)}, u32[]{:S(2)}, u32[]{:S(2)}) async-start(f32[8,1,768]{2,1,0:T(1,128)} %reshape.703), calls=%async_computation.1 | async-start | bytes 49152 | tf_op jit(solution)/shard_map/all_to_all | solution.py:253
  220.0 17.2 %all-to-all-start.2 = ((f32[3,2,32,4]{3,1,0,2:T(2,128)}), f32[3,2,32,4]{3,1,0,2:T(2,128)S(1)}, u32[]{:S(2)}, u32[]{:S(2)}) async-start(f32[3,2,32,4]{3,1,0,2:T(2,128)} %copy.78), calls=%async_computation.2 | async-start | bytes 196608 | tf_op jit(solution)/shard_map/all_to_all | solution.py:255
